TPU v7x, 32 devices: a whole 2x2x4 slice. The times are simulated.
32 devices in a mesh: group: 2 (over x), seq: 8 (over z, y), dp: 2 (over core).
Axes of the slice: x: 2, y: 2, z: 4, core: 2. Of those that a mesh axis runs over, the one named last changes fastest.
Arguments:
- queries: bfloat16 [4, 1024, 512], P(('group', 'dp'), 'seq'), parts along dimension 0, may hold values from -6 to 6
- key_rows: bfloat16 [4, 1024, 512], P(('group', 'dp'), 'seq'), parts along dimension 0, may hold values from -6 to 6
- value_rows: bfloat16 [4, 1024, 768], P(('group', 'dp'), 'seq'), parts along dimension 0, may hold values from -6 to 6
- trunk_state: bfloat16 [4, 1024, 768], P(('group', 'dp'), 'seq'), parts along dimension 0, may hold values from -6 to 6
- skip_input: bfloat16 [4, 2048, 768], P(('group', 'dp'), 'seq'), parts along dimension 0, may hold values from -6 to 6
- norm_gain: bfloat16 [768], replicated, may hold values from 0.099609375 to 1.8984375
- conv_weight: bfloat16 [3840, 384], replicated, may hold values from -0.09375 to 0.09375
- cotangent: bfloat16 [4, 2048, 384], P(('group', 'dp'), 'seq'), parts along dimension 0, may hold values from -6 to 6
Outputs:
- decoded: bfloat16 [4, 2048, 384], P(('group', 'dp'), 'seq'), parts along dimension 0
- grad_queries: bfloat16 [4, 1024, 512], P(('group', 'dp'), 'seq'), parts along dimension 0
- grad_keys: bfloat16 [4, 1024, 512], P(('group', 'dp'), 'seq'), parts along dimension 0
- grad_values: bfloat16 [4, 1024, 768], P(('group', 'dp'), 'seq'), parts along dimension 0
- grad_trunk: bfloat16 [4, 1024, 768], P(('group', 'dp'), 'seq'), parts along dimension 0
- grad_skip: bfloat16 [4, 2048, 768], P(('group', 'dp'), 'seq'), parts along dimension 0
- grad_weight: float32 [7680, 384], P(('group', 'seq', 'dp')), parts along dimension 0
There are 2 independent parts, one for each index of `group`. A program takes and returns all parts, laid end to end along the dimension named above; an argument that names none is the same for every part. Nothing has to cross between parts.
All inputs are finite; a program needn't handle non-finite values.
Results may differ from a plain program's by a relative error of at most 0.029.
Values may be sent and summed in bfloat16 or wider, within the bound.
No kernel may reach another device: no remote copies, remote signals or barrier semaphores. Data moves between devices by JAX's collectives and lax.ppermute only.
A program may use at most 128 MiB of HBM per device.

v0:
```python
import math
import jax
import jax.numpy as jnp
from jax import lax
from jax.sharding import PartitionSpec as P

H = 4
DK = 128
DV = 192
C = 768
CO = 384
KW = 5


def extended(array, sides, width):
    for axis, dim in sides:
        count, length = (lax.axis_size(axis), array.shape[dim])
        up = [(i, (i + 1) % count) for i in range(count - 1)]
        down = [(j, i) for i, j in up]
        last = lax.slice_in_dim(array, length - width, length, axis=dim)
        initial = lax.slice_in_dim(array, 0, width, axis=dim)
        before = lax.ppermute(last, axis, up)
        after = lax.ppermute(initial, axis, down)
        array = jnp.concatenate([before, array, after], axis=dim)
    return array


def gelu_parts(preact):
    cdf_value = 0.5 * (1.0 + jax.scipy.special.erf(preact * (1.0 / math.sqrt(2.0))))
    density = jnp.exp(-0.5 * preact * preact) * (1.0 / math.sqrt(2.0 * math.pi))
    return (preact * cdf_value, cdf_value + preact * density)


def window_rows(padded, kernel, row_count):
    return jnp.concatenate(
        [padded[offset : offset + row_count] for offset in range(kernel)], axis=1
    )


def body(queries, key_rows, value_rows, trunk_state, skip_input, norm_gain, conv_weight, cotangent):
    score_scale = DK ** (-0.5)
    local_tokens = queries.shape[1]
    positions = 2 * local_tokens
    half_kernel = KW // 2
    query_heads = queries[0].reshape(local_tokens, H, DK)
    gathered = (
        lax.all_gather(key_rows, "seq", axis=1, tiled=True),
        lax.all_gather(value_rows, "seq", axis=1, tiled=True),
    )
    all_keys = gathered[0][0].reshape(-1, H, DK)
    all_values = gathered[1][0].reshape(-1, H, DV)
    scores = (
        jnp.einsum("ihd,jhd->hij", query_heads, all_keys, preferred_element_type=jnp.float32)
        * score_scale
    )
    row_peak = jnp.max(scores, axis=2, keepdims=True)
    row_total = jnp.sum(jnp.exp(scores - row_peak), axis=2, keepdims=True)
    logsum = row_peak + jnp.log(row_total)
    softmax = jnp.exp(scores - logsum)
    rounded = softmax.astype(jnp.bfloat16)
    attended = jnp.einsum(
        "hij,jhd->ihd", rounded, all_values, preferred_element_type=jnp.float32
    ).astype(jnp.bfloat16)
    hidden = trunk_state[0].astype(jnp.float32) + attended.reshape(local_tokens, H * DV).astype(
        jnp.float32
    )
    merged = jnp.repeat(hidden, 2, axis=0) + skip_input[0].astype(jnp.float32)
    inverse = lax.rsqrt(jnp.mean(merged * merged, axis=1, keepdims=True) + 1e-06)
    channel_gain = norm_gain.astype(jnp.float32)
    normed = (merged * inverse * channel_gain).astype(jnp.bfloat16)
    padded = extended(normed, (("seq", 0),), half_kernel)
    columns = window_rows(padded, KW, positions)
    preact = jnp.dot(columns, conv_weight, preferred_element_type=jnp.float32)
    activated, derivative = gelu_parts(preact)
    decoded = activated.astype(jnp.bfloat16)
    grad_pre = (cotangent[0].astype(jnp.float32) * derivative).astype(jnp.bfloat16)
    grad_padded = extended(grad_pre, (("seq", 0),), half_kernel)
    norm_scale = (lax.axis_size("dp") * positions * lax.axis_size("seq")) ** (-0.5)
    grad_weight = lax.psum_scatter(
        lax.dot_general(
            columns, grad_pre, (((0,), (0,)), ((), ())), preferred_element_type=jnp.float32
        )
        * norm_scale,
        ("seq", "dp"),
        scatter_dimension=0,
        tiled=True,
    )
    stacked = jnp.stack(
        [
            grad_padded[2 * half_kernel - offset : 2 * half_kernel - offset + positions]
            for offset in range(KW)
        ],
        axis=1,
    )
    weight_blocks = conv_weight.reshape(KW, C, CO)
    grad_normed = jnp.einsum(
        "pko,kco->pc", stacked, weight_blocks, preferred_element_type=jnp.float32
    )
    scaled_grad = grad_normed * channel_gain
    grad_merged = inverse * scaled_grad - merged * inverse**3 * jnp.mean(
        scaled_grad * merged, axis=1, keepdims=True
    )
    grad_skip = grad_merged.astype(jnp.bfloat16)
    grad_trunk = grad_merged.reshape(local_tokens, 2, C).sum(axis=1).astype(jnp.bfloat16)
    grad_heads = grad_trunk.reshape(local_tokens, H, DV)
    row_delta = jnp.sum(grad_heads.astype(jnp.float32) * attended.astype(jnp.float32), axis=2)
    value_grad = jnp.einsum(
        "ihd,jhd->hij", grad_heads, all_values, preferred_element_type=jnp.float32
    )
    slopes = (softmax * (value_grad - row_delta.T[:, :, None])).astype(jnp.bfloat16)
    grad_queries = (
        jnp.einsum("hij,jhd->ihd", slopes, all_keys, preferred_element_type=jnp.float32)
        * score_scale
    ).astype(jnp.bfloat16)
    key_part = (
        jnp.einsum("hij,ihd->jhd", slopes, query_heads, preferred_element_type=jnp.float32)
        * score_scale
    )
    value_part = jnp.einsum("hij,ihd->jhd", rounded, grad_heads, preferred_element_type=jnp.float32)
    summed = lax.psum_scatter(
        jnp.concatenate(
            [
                key_part.reshape(lax.axis_size("seq") * local_tokens, H * DK),
                value_part.reshape(lax.axis_size("seq") * local_tokens, H * DV),
            ],
            axis=1,
        ).astype(jnp.bfloat16),
        "seq",
        scatter_dimension=0,
        tiled=True,
    ).astype(jnp.float32)
    grad_keys = summed[:, : H * DK].astype(jnp.bfloat16)
    grad_values = summed[:, H * DK :].astype(jnp.bfloat16)
    return (
        decoded[None],
        grad_queries.reshape(local_tokens, H * DK)[None],
        grad_keys[None],
        grad_values[None],
        grad_trunk[None],
        grad_skip[None],
        grad_weight,
    )


def solution(mesh):
    return jax.shard_map(
        body,
        mesh=mesh,
        in_specs=(
            P(("group", "dp"), "seq", None),
            P(("group", "dp"), "seq", None),
            P(("group", "dp"), "seq", None),
            P(("group", "dp"), "seq", None),
            P(("group", "dp"), "seq", None),
            P(),
            P(),
            P(("group", "dp"), "seq", None),
        ),
        out_specs=(
            P(("group", "dp"), "seq", None),
            P(("group", "dp"), "seq", None),
            P(("group", "dp"), "seq", None),
            P(("group", "dp"), "seq", None),
            P(("group", "dp"), "seq", None),
            P(("group", "dp"), "seq", None),
            P(("group", "seq", "dp"), None),
        ),
        check_vma=False,
    )
```

profile of v0, /device:TPU:0, one launch (start us, length us, event | category | flops | bytes accessed | tf_op | source)
XLA Modules:
  0.0 324.4 jit_solution(8928119127070148307)
XLA Ops:
  7.2 1.8 copy.24
  11.6 41.2 %all-gather.3.cloned.1.call-done = bf16[1,1024,512]{1,2,0:T(8,128)(2,1)} async-done(((bf16[1,128,512]{1,2,0:T(8,128)(2,1)}), bf16[1,1024,512]{1,2,0:T(8,128)(2,1)}) %all-gather.3.cloned.1.call-update) | async-done | bytes 1048592 | tf_op jit(solution)/shard_map/all_gather | solution.py:47
  52.8 1.8 multiply_reduce_fusion
  54.6 1.3 copy-done.1
  56.4 41.8 %all-gather.5.cloned.1.call-done = bf16[1,1024,768]{2,1,0:T(8,128)(2,1)} async-done(((bf16[1,128,768]{2,1,0:T(8,128)(2,1)}), bf16[1,1024,768]{2,1,0:T(8,128)(2,1)}) %all-gather.5.cloned.1.call-update) | async-done | bytes 1572880 | tf_op jit(solution)/shard_map/all_gather | solution.py:48
  98.2 2.6 copy.27
  100.8 2.8 fusion.2
  106.7 2.6 reshape.93
  109.2 2.6 broadcast_in_dim.26
  111.8 1.3 fusion.6
  113.2 1.3 multiply_convert_fusion.2
  114.5 2.6 collective-permute-start
  117.1 1.3 collective-permute-start.1
  118.6 4.3 %collective-permute-done.1 = bf16[2,768]{1,0:T(2,128)(2,1)S(1)} collective-permute-done((bf16[2,768]{1,0:T(2,128)(2,1)S(1)}, bf16[2,768]{1,0:T(2,128)(2,1)S(1)}, u32[]{:S(2)}, u32[]{:S(2)}) %collective-permute-start.1) | collective-permute-done | bytes 3104 | tf_op jit(solution)/shard_map/ppermute | solution.py:23
  123.1 2.0 fusion.16
  125.2 1.4 collective-permute-start.2
  126.6 5.4 %collective-permute-start.3 = (bf16[2,384]{1,0:T(2,128)(2,1)S(1)}, bf16[2,384]{1,0:T(2,128)(2,1)S(1)}, u32[]{:S(2)}, u32[]{:S(2)}) collective-permute-start(bf16[2,384]{1,0:T(2,128)(2,1)S(1)} %get-tuple-element.27), channel_id=1, source_target_pairs={{0,2},{2,4},{4,6},{6,8},{8,10},{10,12},{12,14},{1,3},{3,5},{5,7},{... | collective-permute-start | bytes 4616 | tf_op jit(solution)/shard_map/ppermute | solution.py:22
  134.6 1.3 convert_bitcast_fusion.1
  135.9 2.5 reshape.95
  138.4 2.8 reduce_sum.48
  141.2 1.7 copy.29
  144.1 3.6 %convolution_convert_fusion = bf16[4,192,1024]{2,1,0:T(8,128)(2,1)} fusion(bf16[128,4,192]{0,2,1:T(8,128)(2,1)} %bitcast.94, f32[4,128,1024]{2,1,0:T(8,128)} %copy-done.1, f32[4,128]{1,0:T(4,128)S(1)} %log_add_fusion), kind=kOutput, calls=%fused_computation.8 | convolution fusion | flops 203685888 | bytes 3868672 | tf_op jit(solution)/shard_map/hij,ihd->jhd/dot_general | solution.py:119
  149.6 1.4 multiply_convert_fusion
  151.0 2.3 copy.31
  153.2 2.6 copy.32
  155.9 3.4 %pad_maximum_fusion = bf16[1024,1280]{1,0:T(8,128)(2,1)} fusion(bf16[1024,768]{1,0:T(8,128)(2,1)} %copy.32, bf16[1024,512]{1,0:T(8,128)(2,1)} %copy.31), kind=kLoop, calls=%fused_computation.1 | loop fusion | flops 5242880 | bytes 5242880 | tf_op jit(solution)/shard_map/concatenate | solution.py:121
  159.3 5.3 %convolution_multiply_fusion = f32[3840,384]{1,0:T(8,128)} fusion(bf16[256,3840]{1,0:T(8,128)(2,1)} %copy-done.7, bf16[256,384]{1,0:T(8,128)(2,1)S(1)} %get-tuple-element.23), kind=kOutput, calls=%fused_computation | convolution fusion | flops 756449280 | bytes 8060928 | tf_op jit(solution)/shard_map/dot_general | solution.py:80
  164.7 2.0 fusion.3
  167.4 64.6 %reduce-scatter.3.cloned.1.call-done = bf16[128,1280]{1,0:T(8,128)(2,1)} async-done(((bf16[1024,1280]{1,0:T(8,128)(2,1)}), bf16[128,1280]{1,0:T(8,128)(2,1)}) %reduce-scatter.3.cloned.1.call-update) | async-done | bytes 327696 | tf_op jit(solution)/shard_map/reduce_scatter | solution.py:120
  232.0 1.6 slice_bitcast_fusion.1
  233.6 1.6 slice_bitcast_fusion
  235.2 82.7 %reduce-scatter.5.cloned.1.call-done = f32[240,384]{1,0:T(8,128)} async-done(((f32[3840,384]{1,0:T(8,128)}), f32[240,384]{1,0:T(8,128)}) %reduce-scatter.5.cloned.1.call-update) | async-done | bytes 368656 | tf_op jit(solution)/shard_map/reduce_scatter | solution.py:79
  (65 shorter events, 13.0 us)
Async XLA Ops:
  7.2 115.9 %copy-start = (bf16[3840,384]{1,0:T(8,128)(2,1)S(1)}, bf16[3840,384]{1,0:T(8,128)(2,1)}, u32[]{:S(2)}) copy-start(bf16[3840,384]{1,0:T(8,128)(2,1)} %param.14) | copy-start | bytes 8847364
  7.2 45.6 %all-gather.3.cloned.1.call-start = ((), (), s32[]{:S(2)}) async-start(), calls=%async_computation.2 | async-start | bytes 1179648 | tf_op jit(solution)/shard_map/all_gather | solution.py:47
  9.1 89.1 %all-gather.5.cloned.1.call-start = ((), (), s32[]{:S(2)}) async-start(), calls=%async_computation.3 | async-start | bytes 1769472 | tf_op jit(solution)/shard_map/all_gather | solution.py:48
  9.8 222.2 %reduce-scatter.3.cloned.1.call-start = ((), (), s32[]{:S(2)}) async-start(), calls=%async_computation.4 | async-start | bytes 2949120 | tf_op jit(solution)/shard_map/reduce_scatter | solution.py:120
  11.6 44.8 %copy-start.11 = (bf16[1,128,512]{1,2,0:T(8,128)(2,1)}, bf16[1,128,512]{1,2,0:T(8,128)(2,1)S(1)}, u32[]{:S(2)}) copy-start(bf16[1,128,512]{1,2,0:T(8,128)(2,1)S(1)} %copy.35) | copy-start | bytes 393220
  54.5 1.3 copy-start.1
  100.8 3.7 %copy-start.13 = (bf16[1,128,768]{2,1,0:T(8,128)(2,1)S(1)}, bf16[1,128,768]{2,1,0:T(8,128)(2,1)}, u32[]{:S(2)}) copy-start(bf16[1,128,768]{2,1,0:T(8,128)(2,1)} %param.11) | copy-start | bytes 589828
  103.5 0.9 copy-start.8
  105.5 6.3 %copy-start.6 = (bf16[1,256,768]{2,1,0:T(8,128)(2,1)S(1)}, bf16[1,256,768]{2,1,0:T(8,128)(2,1)}, u32[]{:S(2)}) copy-start(bf16[1,256,768]{2,1,0:T(8,128)(2,1)} %param.12) | copy-start | bytes 1179652
  114.4 8.7 %copy-start.14 = (bf16[1,256,384]{2,1,0:T(8,128)(2,1)S(1)}, bf16[1,256,384]{2,1,0:T(8,128)(2,1)}, u32[]{:S(2)}) copy-start(bf16[1,256,384]{2,1,0:T(8,128)(2,1)} %param.15) | copy-start | bytes 589828
  114.5 3.9 %collective-permute-start = (bf16[2,768]{1,0:T(2,128)(2,1)S(1)}, bf16[2,768]{1,0:T(2,128)(2,1)S(1)}, u32[]{:S(2)}, u32[]{:S(2)}) collective-permute-start(bf16[2,768]{1,0:T(2,128)(2,1)S(1)} %get-tuple-element.26), channel_id=1, source_target_pairs={{0,2},{2,4},{4,6},{6,8},{8,10},{10,12},{12,14},{1,3},{3,5},{5,7},{... | collective-permute-start | bytes 9224 | tf_op jit(solution)/shard_map/ppermute | solution.py:22
  117.1 5.8 %collective-permute-start.1 = (bf16[2,768]{1,0:T(2,128)(2,1)S(1)}, bf16[2,768]{1,0:T(2,128)(2,1)S(1)}, u32[]{:S(2)}, u32[]{:S(2)}) collective-permute-start(bf16[2,768]{1,0:T(2,128)(2,1)S(1)} %get-tuple-element.25), channel_id=1, source_target_pairs={{2,0},{4,2},{6,4},{8,6},{10,8},{12,10},{14,12},{3,1},{5,3},{7,5},{... | collective-permute-start | bytes 9224 | tf_op jit(solution)/shard_map/ppermute | solution.py:23
  123.1 2.0 copy-start.7
  125.1 8.3 %copy-start.4 = (f32[256,768]{1,0:T(8,128)S(1)}, f32[256,768]{1,0:T(8,128)}, u32[]{:S(2)}) copy-start(f32[256,768]{1,0:T(8,128)} %reshape.93) | copy-start | bytes 2359300
  125.2 6.9 %collective-permute-start.2 = (bf16[2,384]{1,0:T(2,128)(2,1)S(1)}, bf16[2,384]{1,0:T(2,128)(2,1)S(1)}, u32[]{:S(2)}, u32[]{:S(2)}) collective-permute-start(bf16[2,384]{1,0:T(2,128)(2,1)S(1)} %get-tuple-element.28), channel_id=1, source_target_pairs={{2,0},{4,2},{6,4},{8,6},{10,8},{12,10},{14,12},{3,1},{5,3},{7,5},{... | collective-permute-start | bytes 4616 | tf_op jit(solution)/shard_map/ppermute | solution.py:23
  126.6 6.7 %collective-permute-start.3 = (bf16[2,384]{1,0:T(2,128)(2,1)S(1)}, bf16[2,384]{1,0:T(2,128)(2,1)S(1)}, u32[]{:S(2)}, u32[]{:S(2)}) collective-permute-start(bf16[2,384]{1,0:T(2,128)(2,1)S(1)} %get-tuple-element.27), channel_id=1, source_target_pairs={{0,2},{2,4},{4,6},{6,8},{8,10},{10,12},{12,14},{1,3},{3,5},{5,7},{... | collective-permute-start | bytes 4616 | tf_op jit(solution)/shard_map/ppermute | solution.py:22
  135.9 7.0 %copy-start.9 = (f32[4,128,192]{1,2,0:T(8,128)S(1)}, f32[4,128,192]{1,2,0:T(8,128)}, u32[]{:S(2)}) copy-start(f32[4,128,192]{1,2,0:T(8,128)} %copy-done.8) | copy-start | bytes 1179652
  142.9 4.8 %copy-start.2 = (f32[4,128,1024]{2,1,0:T(8,128)S(1)}, f32[4,128,1024]{2,1,0:T(8,128)}, u32[]{:S(2)}) copy-start(f32[4,128,1024]{2,1,0:T(8,128)} %copy-done.1) | copy-start | bytes 6291460
  142.9 4.8 %copy-start.3 = (bf16[1,1024,768]{1,2,0:T(8,128)(2,1)S(1)}, bf16[1,1024,768]{1,2,0:T(8,128)(2,1)}, u32[]{:S(2)}) copy-start(bf16[1,1024,768]{1,2,0:T(8,128)(2,1)} %copy.27) | copy-start | bytes 4718596
  142.9 4.8 %copy-start.10 = (bf16[128,768]{0,1:T(8,128)(2,1)S(1)}, bf16[128,768]{0,1:T(8,128)(2,1)}, u32[]{:S(2)}) copy-start(bf16[128,768]{0,1:T(8,128)(2,1)} %copy.29) | copy-start | bytes 589828
  147.7 1.9 copy-start.12
  148.6 1.0 copy-start.5
  159.3 158.6 %reduce-scatter.5.cloned.1.call-start = ((), (), s32[]{:S(2)}) async-start(), calls=%async_computation.5 | async-start | bytes 6266880 | tf_op jit(solution)/shard_map/reduce_scatter | solution.py:79
Sparse Core Ops, SparseCore 0:
  10.6 42.1 all-gather.2
  54.9 43.1 all-gather.4
  159.4 72.5 reduce-scatter.2
  236.4 81.4 reduce-scatter.4
where the time goes:
time: 325 us; the launch traced here: 324 us
  waiting for transfers between devices  236 us (73%)
  local copies, waits for them, and re-layouts  28.3 us (9%)
  matrix products  20.8 us (6%)
  other arithmetic  14 us (4%)
  between operations  14 us (4%)
  starting transfers between devices  10.9 us (3%)
    reduce_scatter x1, waiting for transfers between devices, body(): lax.psum_scatter(lax.dot_general(columns, grad_pre, (((0,), (0,)), ((), (...  82.7 us
    reduce_scatter x1, waiting for transfers between devices, body(): lax.psum_scatter(jnp.concatenate([key_part.reshape(lax.axis_size('seq') *...  64.6 us
    all_gather x1, waiting for transfers between devices, body(): lax.all_gather(value_rows, 'seq', axis=1, tiled=True)  41.8 us
    all_gather x1, waiting for transfers between devices, body(): lax.all_gather(key_rows, 'seq', axis=1, tiled=True)  41.2 us
    ppermute x2, starting transfers between devices, extended(): before = lax.ppermute(last, axis, up)  8.03 us
  transfers between devices with their start and end apart: 8, of which 6 were waited for; matrix products, arithmetic and copies ran while one was open for 5% of the time, Pallas kernels for 0%

commit v1 on v0

--- a/solution.py
+++ b/solution.py
@@ -10,6 +10,27 @@
 C = 768
 CO = 384
 KW = 5
+
+
+def tokens_touch(v0, pos_dim):
+    v0 = jnp.moveaxis(v0, 0, pos_dim)
+    e_now = v0.shape
+    val = v0.reshape(*e_now[:pos_dim], e_now[pos_dim] * e_now[pos_dim + 1], *e_now[pos_dim + 2 :])
+    return val
+
+
+def cut_the_teams(my_tile, row_axis):
+    n_parts = lax.axis_size(row_axis)
+    spare = my_tile[None]
+    for num in range(n_parts.bit_length() - 1):
+        item_now = 1 << num
+        f_now = lax.ppermute(
+            spare, row_axis, perm=list(map(lambda p: (p, p ^ item_now), range(n_parts)))
+        )
+        x_next = jnp.stack([spare, f_now], 0)
+        e_next = lax.axis_index(row_axis) >> num & 1
+        spare = jnp.where(e_next == 0, x_next, x_next[::-1]).reshape(-1, *my_tile.shape)
+    return spare
 
 
 def extended(array, sides, width):
@@ -43,9 +64,15 @@
     positions = 2 * local_tokens
     half_kernel = KW // 2
     query_heads = queries[0].reshape(local_tokens, H, DK)
+
+    def pair_face(x_part, k_dim, t0):
+        front = cut_the_teams(t0, x_part)
+        view_out = tokens_touch(front, k_dim)
+        return view_out
+
     gathered = (
         lax.all_gather(key_rows, "seq", axis=1, tiled=True),
-        lax.all_gather(value_rows, "seq", axis=1, tiled=True),
+        pair_face("seq", 1, value_rows),
     )
     all_keys = gathered[0][0].reshape(-1, H, DK)
     all_values = gathered[1][0].reshape(-1, H, DV)

time: 325 us -> 309 us (0.951)
  waiting for transfers between devices: 236 us -> 206 us
  starting transfers between devices: 10.9 us -> 18.8 us
  other arithmetic: 14 us -> 20.2 us
    ppermute x0 -> x3, waiting for transfers between devices: none -> 53.6 us  [cut_the_teams(): lax.ppermute(spare, row_axis, perm=list(map(lambda p: (p, p ^ item_now),...]
    all_gather x1 -> x0, waiting for transfers between devices: 41.8 us -> none  [body(): lax.all_gather(value_rows, 'seq', axis=1, tiled=True)]
    all_gather x1, waiting for transfers between devices: 41.2 us -> 0.01 us  [body(): lax.all_gather(key_rows, 'seq', axis=1, tiled=True)]
    ppermute x0 -> x3, starting transfers between devices: none -> 7.39 us  [cut_the_teams(): lax.ppermute(spare, row_axis, perm=list(map(lambda p: (p, p ^ item_now),...]
    another operation x0 -> x4, other arithmetic: none -> 4.38 us  [cut_the_teams(): x_next = jnp.stack([spare, f_now], 0)]
    select_n x0 -> x1, local copies, waits for them, and re-layouts: none -> 3.81 us  [cut_the_teams(): jnp.where(e_next == 0, x_next, x_next[::-1]).reshape(-1, *my_tile.shape)]
    another operation x0 -> x1, local copies, waits for them, and re-layouts: none -> 3.79 us  [body(): all_values = gathered[1][0].reshape(-1, H, DV)]
  transfers between devices with their start and end apart: 8 -> 10, of which waited for: 6 -> 7; matrix products, arithmetic and copies ran while one was open for 5% -> 8% of each run, Pallas kernels for 0% -> 0%
where the time goes in v1:
time: 309 us
  waiting for transfers between devices  206 us (67%)
  local copies, waits for them, and re-layouts  30.9 us (10%)
  other arithmetic  20.2 us (7%)
  matrix products  18.9 us (6%)
  starting transfers between devices  18.8 us (6%)
  between operations  14.1 us (5%)
    reduce_scatter x1, waiting for transfers between devices, body(): lax.psum_scatter(lax.dot_general(columns, grad_pre, (((0,), (0,)), ((), (...  82.9 us
    reduce_scatter x1, waiting for transfers between devices, body(): lax.psum_scatter(jnp.concatenate([key_part.reshape(lax.axis_size('seq') *...  64.3 us
    ppermute x3, waiting for transfers between devices, cut_the_teams(): lax.ppermute(spare, row_axis, perm=list(map(lambda p: (p, p ^ item_now),...  53.6 us
    ppermute x2, starting transfers between devices, extended(): before = lax.ppermute(last, axis, up)  8.55 us
    ppermute x3, starting transfers between devices, cut_the_teams(): lax.ppermute(spare, row_axis, perm=list(map(lambda p: (p, p ^ item_now),...  7.39 us
  transfers between devices with their start and end apart: 10, of which 7 were waited for; matrix products, arithmetic and copies ran while one was open for 8% of the time, Pallas kernels for 0%

profile of v1, /device:TPU:0, one launch (start us, length us, event | category | flops | bytes accessed | tf_op | source)
XLA Modules:
  0.0 308.5 jit_solution(8900866746862414155)
XLA Ops:
  7.2 3.1 collective-permute-start
  10.3 5.1 %collective-permute-done = bf16[1,1,128,768]{3,2,1,0:T(8,128)(2,1)S(1)} collective-permute-done((bf16[1,1,128,768]{3,2,1,0:T(8,128)(2,1)}, bf16[1,1,128,768]{3,2,1,0:T(8,128)(2,1)S(1)}, u32[]{:S(2)}, u32[]{:S(2)}) %collective-permute-start) | collective-permute-done | bytes 196640 | tf_op jit(solution)/shard_map/ppermute | solution.py:27
  17.2 1.8 collective-permute-start.1
  19.0 1.7 copy.25
  20.8 7.1 %collective-permute-done.1 = bf16[2,1,128,768]{3,2,0,1:T(8,128)(2,1)} collective-permute-done((bf16[2,1,128,768]{3,2,0,1:T(8,128)(2,1)}, bf16[2,1,128,768]{3,2,0,1:T(8,128)(2,1)}, u32[]{:S(2)}, u32[]{:S(2)}) %collective-permute-start.1) | collective-permute-done | bytes 393248 | tf_op jit(solution)/shard_map/ppermute | solution.py:27
  29.9 2.5 collective-permute-start.2
  32.6 41.4 %collective-permute-done.2 = bf16[4,1,128,768]{3,2,0,1:T(8,128)(2,1)} collective-permute-done((bf16[4,1,128,768]{3,2,0,1:T(8,128)(2,1)}, bf16[4,1,128,768]{3,2,0,1:T(8,128)(2,1)}, u32[]{:S(2)}, u32[]{:S(2)}) %collective-permute-start.2) | collective-permute-done | bytes 786464 | tf_op jit(solution)/shard_map/ppermute | solution.py:27
  74.0 1.5 pad_maximum_fusion.1
  75.5 1.4 reverse_select_fusion
  77.0 3.8 %copy.24 = bf16[2,4,1,128,768]{3,1,0,4,2:T(4,128)(2,1)} copy(bf16[2,4,1,128,768]{4,3,1,2,0:T(8,128)(2,1)} %reverse_select_fusion) | data formatting | bytes 3145728 | tf_op jit(solution)/shard_map/jit(_where)/select_n | solution.py:32
  80.8 3.8 %reshape_squeeze_reshape_transpose_reshape.3 = bf16[1024,4,192]{0,2,1:T(8,128)(2,1)} reshape(bf16[2,4,1,128,768]{3,1,0,4,2:T(4,128)(2,1)} %copy.24) | data formatting | bytes 3145728 | tf_op jit(solution)/shard_map/reshape;squeeze;reshape;transpose;reshape | solution.py:78
  84.6 1.9 multiply_reduce_fusion
  90.9 2.6 reshape.101
  93.5 2.6 broadcast_in_dim.30
  98.7 3.8 %collective-permute-start.3 = (bf16[2,768]{1,0:T(2,128)(2,1)S(1)}, bf16[2,768]{1,0:T(2,128)(2,1)S(1)}, u32[]{:S(2)}, u32[]{:S(2)}) collective-permute-start(bf16[2,768]{1,0:T(2,128)(2,1)S(1)} %get-tuple-element.26), channel_id=1, source_target_pairs={{0,2},{2,4},{4,6},{6,8},{8,10},{10,12},{12,14},{1,3},{3,5},{5,7},{... | collective-permute-start | bytes 9224 | tf_op jit(solution)/shard_map/ppermute | solution.py:43
  104.1 3.9 %collective-permute-done.4 = bf16[2,768]{1,0:T(2,128)(2,1)S(1)} collective-permute-done((bf16[2,768]{1,0:T(2,128)(2,1)S(1)}, bf16[2,768]{1,0:T(2,128)(2,1)S(1)}, u32[]{:S(2)}, u32[]{:S(2)}) %collective-permute-start.4) | collective-permute-done | bytes 3104 | tf_op jit(solution)/shard_map/ppermute | solution.py:44
  108.3 2.0 fusion.16
  110.3 1.4 collective-permute-start.5
  111.8 4.7 %collective-permute-start.6 = (bf16[2,384]{1,0:T(2,128)(2,1)S(1)}, bf16[2,384]{1,0:T(2,128)(2,1)S(1)}, u32[]{:S(2)}, u32[]{:S(2)}) collective-permute-start(bf16[2,384]{1,0:T(2,128)(2,1)S(1)} %get-tuple-element.29), channel_id=1, source_target_pairs={{0,2},{2,4},{4,6},{6,8},{8,10},{10,12},{12,14},{1,3},{3,5},{5,7},{... | collective-permute-start | bytes 4616 | tf_op jit(solution)/shard_map/ppermute | solution.py:43
  120.1 2.5 reshape.103
  122.7 2.8 reduce_sum.48
  125.4 1.7 copy.29
  128.3 3.6 %convolution_convert_fusion = bf16[4,192,1024]{2,1,0:T(8,128)(2,1)} fusion(bf16[128,4,192]{0,2,1:T(8,128)(2,1)} %bitcast.104, f32[4,128,1024]{2,1,0:T(8,128)} %copy-done.1, f32[4,128]{1,0:T(4,128)S(1)} %log_add_fusion), kind=kOutput, calls=%fused_computation.9 | convolution fusion | flops 203685888 | bytes 3868672 | tf_op jit(solution)/shard_map/hij,ihd->jhd/dot_general | solution.py:146
  135.2 2.3 copy.31
  137.5 2.6 copy.32
  140.1 3.4 %pad_maximum_fusion = bf16[1024,1280]{1,0:T(8,128)(2,1)} fusion(bf16[1024,768]{1,0:T(8,128)(2,1)} %copy.32, bf16[1024,512]{1,0:T(8,128)(2,1)} %copy.31), kind=kLoop, calls=%fused_computation.1 | loop fusion | flops 5242880 | bytes 5242880 | tf_op jit(solution)/shard_map/concatenate | solution.py:148
  143.6 5.3 %convolution_multiply_fusion = f32[3840,384]{1,0:T(8,128)} fusion(bf16[256,3840]{1,0:T(8,128)(2,1)} %copy-done.8, bf16[256,384]{1,0:T(8,128)(2,1)S(1)} %get-tuple-element.23), kind=kOutput, calls=%fused_computation | convolution fusion | flops 756449280 | bytes 8060928 | tf_op jit(solution)/shard_map/dot_general | solution.py:107
  148.9 2.0 fusion.3
  151.7 64.3 %reduce-scatter.3.cloned.1.call-done = bf16[128,1280]{1,0:T(8,128)(2,1)} async-done(((bf16[1024,1280]{1,0:T(8,128)(2,1)}), bf16[128,1280]{1,0:T(8,128)(2,1)}) %reduce-scatter.3.cloned.1.call-update) | async-done | bytes 327696 | tf_op jit(solution)/shard_map/reduce_scatter | solution.py:147
  216.0 1.6 slice_bitcast_fusion.1
  217.5 1.6 slice_bitcast_fusion
  219.1 82.9 %reduce-scatter.5.cloned.1.call-done = f32[240,384]{1,0:T(8,128)} async-done(((f32[3840,384]{1,0:T(8,128)}), f32[240,384]{1,0:T(8,128)}) %reduce-scatter.5.cloned.1.call-update) | async-done | bytes 368656 | tf_op jit(solution)/shard_map/reduce_scatter | solution.py:106
  (81 shorter events, 21.7 us)
Async XLA Ops:
  7.2 101.1 %copy-start = (bf16[3840,384]{1,0:T(8,128)(2,1)S(1)}, bf16[3840,384]{1,0:T(8,128)(2,1)}, u32[]{:S(2)}) copy-start(bf16[3840,384]{1,0:T(8,128)(2,1)} %param.14) | copy-start | bytes 8847364
  7.2 77.4 %all-gather.2.cloned.1.call-start = ((), (), s32[]{:S(2)}) async-start(), calls=%async_computation.2 | async-start | bytes 1179648 | tf_op jit(solution)/shard_map/all_gather | solution.py:74
  7.2 8.2 %collective-permute-start = (bf16[1,1,128,768]{3,2,1,0:T(8,128)(2,1)}, bf16[1,1,128,768]{3,2,1,0:T(8,128)(2,1)S(1)}, u32[]{:S(2)}, u32[]{:S(2)}) collective-permute-start(bf16[1,1,128,768]{3,2,1,0:T(8,128)(2,1)} %bitcast.110), channel_id=1, source_target_pairs={{0,2},{2,0},{4,6},{6,4},{8,10},{10,8},{12,14},{14,12},{1,3},{3,1},... | collective-permute-start | bytes 589832 | tf_op jit(solution)/shard_map/ppermute | solution.py:27
  16.4 16.1 %copy-start.16 = (bf16[768]{0:T(1024)(128)(2,1)S(1)}, bf16[768]{0:T(1024)(128)(2,1)}, u32[]{:S(2)}) copy-start(bf16[768]{0:T(1024)(128)(2,1)} %param.13) | copy-start | bytes 4612
  16.4 16.1 %copy-start.15 = (bf16[1,128,512]{2,1,0:T(8,128)(2,1)S(1)}, bf16[1,128,512]{2,1,0:T(8,128)(2,1)}, u32[]{:S(2)}) copy-start(bf16[1,128,512]{2,1,0:T(8,128)(2,1)} %param.8) | copy-start | bytes 393220
  17.2 10.6 %collective-permute-start.1 = (bf16[2,1,128,768]{3,2,0,1:T(8,128)(2,1)}, bf16[2,1,128,768]{3,2,0,1:T(8,128)(2,1)}, u32[]{:S(2)}, u32[]{:S(2)}) collective-permute-start(bf16[2,1,128,768]{3,2,0,1:T(8,128)(2,1)} %get-tuple-element.28), channel_id=1, source_target_pairs={{0,4},{2,6},{4,0},{6,2},{8,12},{10,14},{12,8},{14,10},{1,5},{3,7},... | collective-permute-start | bytes 1179656 | tf_op jit(solution)/shard_map/ppermute | solution.py:27
  20.7 195.3 %reduce-scatter.3.cloned.1.call-start = ((), (), s32[]{:S(2)}) async-start(), calls=%async_computation.3 | async-start | bytes 2949120 | tf_op jit(solution)/shard_map/reduce_scatter | solution.py:147
  29.9 44.1 %collective-permute-start.2 = (bf16[4,1,128,768]{3,2,0,1:T(8,128)(2,1)}, bf16[4,1,128,768]{3,2,0,1:T(8,128)(2,1)}, u32[]{:S(2)}, u32[]{:S(2)}) collective-permute-start(bf16[4,1,128,768]{3,2,0,1:T(8,128)(2,1)} %bitcast.8), channel_id=1, source_target_pairs={{0,8},{2,10},{4,12},{6,14},{8,0},{10,2},{12,4},{14,6},{1,9},{3,11}... | collective-permute-start | bytes 2359304 | tf_op jit(solution)/shard_map/ppermute | solution.py:27
  32.6 52.0 %copy-start.12 = (bf16[1,128,512]{1,2,0:T(8,128)(2,1)}, bf16[1,128,512]{1,2,0:T(8,128)(2,1)S(1)}, u32[]{:S(2)}) copy-start(bf16[1,128,512]{1,2,0:T(8,128)(2,1)S(1)} %copy.35) | copy-start | bytes 393220
  84.6 2.4 copy-start.3
  86.5 1.3 copy-start.1
  87.0 1.7 copy-start.14
  87.8 0.9 copy-start.9
  89.8 6.3 %copy-start.7 = (bf16[1,256,768]{2,1,0:T(8,128)(2,1)S(1)}, bf16[1,256,768]{2,1,0:T(8,128)(2,1)}, u32[]{:S(2)}) copy-start(bf16[1,256,768]{2,1,0:T(8,128)(2,1)} %param.12) | copy-start | bytes 1179652
  98.7 9.6 %copy-start.17 = (bf16[1,256,384]{2,1,0:T(8,128)(2,1)S(1)}, bf16[1,256,384]{2,1,0:T(8,128)(2,1)}, u32[]{:S(2)}) copy-start(bf16[1,256,384]{2,1,0:T(8,128)(2,1)} %param.15) | copy-start | bytes 589828
  98.7 5.1 %collective-permute-start.3 = (bf16[2,768]{1,0:T(2,128)(2,1)S(1)}, bf16[2,768]{1,0:T(2,128)(2,1)S(1)}, u32[]{:S(2)}, u32[]{:S(2)}) collective-permute-start(bf16[2,768]{1,0:T(2,128)(2,1)S(1)} %get-tuple-element.26), channel_id=1, source_target_pairs={{0,2},{2,4},{4,6},{6,8},{8,10},{10,12},{12,14},{1,3},{3,5},{5,7},{... | collective-permute-start | bytes 9224 | tf_op jit(solution)/shard_map/ppermute | solution.py:43
  102.6 5.5 %collective-permute-start.4 = (bf16[2,768]{1,0:T(2,128)(2,1)S(1)}, bf16[2,768]{1,0:T(2,128)(2,1)S(1)}, u32[]{:S(2)}, u32[]{:S(2)}) collective-permute-start(bf16[2,768]{1,0:T(2,128)(2,1)S(1)} %get-tuple-element.25), channel_id=1, source_target_pairs={{2,0},{4,2},{6,4},{8,6},{10,8},{12,10},{14,12},{3,1},{5,3},{7,5},{... | collective-permute-start | bytes 9224 | tf_op jit(solution)/shard_map/ppermute | solution.py:44
  108.3 2.0 copy-start.8
  110.3 7.4 %copy-start.5 = (f32[256,768]{1,0:T(8,128)S(1)}, f32[256,768]{1,0:T(8,128)}, u32[]{:S(2)}) copy-start(f32[256,768]{1,0:T(8,128)} %reshape.101) | copy-start | bytes 2359300
  110.3 6.2 %collective-permute-start.5 = (bf16[2,384]{1,0:T(2,128)(2,1)S(1)}, bf16[2,384]{1,0:T(2,128)(2,1)S(1)}, u32[]{:S(2)}, u32[]{:S(2)}) collective-permute-start(bf16[2,384]{1,0:T(2,128)(2,1)S(1)} %get-tuple-element.30), channel_id=1, source_target_pairs={{2,0},{4,2},{6,4},{8,6},{10,8},{12,10},{14,12},{3,1},{5,3},{7,5},{... | collective-permute-start | bytes 4616 | tf_op jit(solution)/shard_map/ppermute | solution.py:44
  111.8 5.8 %collective-permute-start.6 = (bf16[2,384]{1,0:T(2,128)(2,1)S(1)}, bf16[2,384]{1,0:T(2,128)(2,1)S(1)}, u32[]{:S(2)}, u32[]{:S(2)}) collective-permute-start(bf16[2,384]{1,0:T(2,128)(2,1)S(1)} %get-tuple-element.29), channel_id=1, source_target_pairs={{0,2},{2,4},{4,6},{6,8},{8,10},{10,12},{12,14},{1,3},{3,5},{5,7},{... | collective-permute-start | bytes 4616 | tf_op jit(solution)/shard_map/ppermute | solution.py:43
  120.1 7.0 %copy-start.10 = (f32[4,192,128]{2,1,0:T(8,128)S(1)}, f32[4,192,128]{2,1,0:T(8,128)}, u32[]{:S(2)}) copy-start(f32[4,192,128]{2,1,0:T(8,128)} %copy-done.9) | copy-start | bytes 1179652
  127.2 4.8 %copy-start.2 = (f32[4,128,1024]{2,1,0:T(8,128)S(1)}, f32[4,128,1024]{2,1,0:T(8,128)}, u32[]{:S(2)}) copy-start(f32[4,128,1024]{2,1,0:T(8,128)} %copy-done.1) | copy-start | bytes 6291460
  127.2 4.8 %copy-start.4 = (bf16[1024,4,192]{0,2,1:T(8,128)(2,1)S(1)}, bf16[1024,4,192]{0,2,1:T(8,128)(2,1)}, u32[]{:S(2)}) copy-start(bf16[1024,4,192]{0,2,1:T(8,128)(2,1)} %reshape_squeeze_reshape_transpose_reshape.3) | copy-start | bytes 4718596
  127.2 4.8 %copy-start.11 = (bf16[128,768]{0,1:T(8,128)(2,1)S(1)}, bf16[128,768]{0,1:T(8,128)(2,1)}, u32[]{:S(2)}) copy-start(bf16[128,768]{0,1:T(8,128)(2,1)} %copy.29) | copy-start | bytes 589828
  132.0 1.8 copy-start.13
  132.8 1.0 copy-start.6
  143.5 158.5 %reduce-scatter.5.cloned.1.call-start = ((), (), s32[]{:S(2)}) async-start(), calls=%async_computation.4 | async-start | bytes 6266880 | tf_op jit(solution)/shard_map/reduce_scatter | solution.py:106
Sparse Core Ops, SparseCore 0:
  20.8 62.1 all-gather.1
  143.7 72.2 reduce-scatter.2
  220.5 81.4 reduce-scatter.4
